TPU v7x, 32 devices: a whole 2x2x4 slice. The times are simulated.
32 devices in a mesh: dom: 2 (over y), blk: 16 (over z, x, core).
Axes of the slice: x: 2, y: 2, z: 4, core: 2. Of those that a mesh axis runs over, the one named last changes fastest.
Arguments:
- right_side: float32 [2, 4, 2, 8192], P(None, None, 'dom', 'blk')
- near_blocks: bfloat16 [2, 32, 4, 2, 256, 256], P('dom', 'blk'), may hold values from -0.125 to 0.125
- near_cols: int32 [2, 32, 4], P('dom', 'blk'), may hold values from 0 to 5
- partner: int32 [2, 32], P('dom', 'blk'), may hold values from 0 to 3, as said below
- source_basis: bfloat16 [2, 2, 64, 8192], P('dom', None, None, 'blk'), may hold values from -0.25 to 0.25
- target_basis: bfloat16 [2, 2, 64, 8192], P('dom', None, None, 'blk'), may hold values from -0.75 to 0.75
- coupling: float32 [2, 16, 16, 2, 64, 64], P('dom', 'blk'), as said below
- far_ranks: int32 [2, 16, 16], P('dom', 'blk'), may hold values from 32 to 64, as said below
Outputs:
- second_basis: float32 [2, 4, 2, 8192], P(None, None, 'dom', 'blk')
- third_basis: float32 [2, 4, 2, 8192], P(None, None, 'dom', 'blk')
- hessenberg: float32 [4, 9], replicated
Inputs may be any that keep to these rules, and one draw needn't show every extreme that they name: partner[d, c * 2 + i] = e * 2 + j names block j of cluster c in subdomain e; the named block names the first one back, and no block names itself. coupling[d, c, s, a, k, l] equals coupling[d, s, c, a, l, k]. far_ranks[d, c, s] equals far_ranks[d, s, c].
All inputs are finite; a program needn't handle non-finite values.
Results may differ from a plain program's by a relative error of at most 0.0065.
Values may be sent and summed in bfloat16 or wider, within the bound.
No kernel may reach another device: no remote copies, remote signals or barrier semaphores. Data moves between devices by JAX's collectives and lax.ppermute only.
A program may use at most 64 MiB of HBM per device.

v0:
```python
import jax
import jax.numpy as jnp
from jax import lax
from jax.sharding import PartitionSpec as P

EPSILON = 1e-06


def extended(cells, sides, width):
    for axis, dim in sides:
        count = lax.axis_size(axis)
        ends = count - 1
        head = lax.slice_in_dim(cells, 0, width, axis=dim)
        tail = lax.slice_in_dim(cells, cells.shape[dim] - width, cells.shape[dim], axis=dim)
        cells = jnp.concatenate(
            [
                lax.ppermute(tail, axis, [(i, (i + 1) % count) for i in range(ends)]),
                cells,
                lax.ppermute(head, axis, [((i + 1) % count, i) for i in range(ends)]),
            ],
            axis=dim,
        )
    return cells


def complex_mix(products):
    return jnp.stack([products[0, 0] - products[1, 1], products[0, 1] + products[1, 0]])


def apply_operator(
    vector, near_blocks, near_cols, partner, source_basis, target_basis, coupling, far_ranks
):
    nrhs = vector.shape[1]
    rows = vector.shape[3]
    blocks_dev = near_blocks.shape[1]
    slots = near_blocks.shape[2]
    width = near_blocks.shape[4]
    rank_cap = source_basis.shape[2]
    rounded = vector.astype(jnp.bfloat16)
    window = extended(rounded, (("blk", 3),), rows)
    window = window.reshape(2, nrhs, 3 * blocks_dev, width)
    chosen = jnp.take(window, near_cols[0].reshape(-1), axis=2).reshape(
        2, nrhs, blocks_dev, slots, width
    )
    near_prod = jnp.einsum(
        "ikarc,pqikc->apqir", near_blocks[0], chosen, preferred_element_type=jnp.float32
    )
    near_part = complex_mix(near_prod).reshape(2, nrhs, 1, rows)
    coef_prod = jnp.einsum(
        "akr,pqr->apqk", source_basis[0], rounded[:, :, 0], preferred_element_type=jnp.float32
    )
    coeffs = jnp.stack([coef_prod[0, 0] + coef_prod[1, 1], coef_prod[0, 1] - coef_prod[1, 0]])
    row_coupling = coupling[0, 0]
    row_ranks = far_ranks[0, 0]
    levels = jnp.arange(rank_cap, dtype=jnp.int32)
    limit = row_ranks[:, None, None]
    keep = (levels[None, :, None] < limit) & (levels[None, None, :] < limit)
    weights = row_coupling * keep[:, None].astype(jnp.float32)
    inner = jnp.einsum(
        "sakl,spql->apqk",
        weights,
        lax.all_gather(coeffs[None], "blk", axis=0, tiled=True),
        precision=lax.Precision.HIGHEST,
    )
    far_coef = complex_mix(inner)
    rounded_coef = far_coef.astype(jnp.bfloat16)
    outward = jnp.einsum(
        "akr,pqk->apqr", target_basis[0], rounded_coef, preferred_element_type=jnp.float32
    )
    far_part = complex_mix(outward).reshape(2, nrhs, 1, rows)
    every = lax.all_gather(vector, "dom", axis=2, tiled=True)
    every = every.reshape(2, nrhs, -1, width)
    mates = jnp.take(every, partner[0], axis=2).reshape(2, nrhs, 1, rows)
    return vector + near_part + far_part - mates


def local_products(vectors, image):
    stacked = []
    for basis in vectors:
        real_part = jnp.sum(basis[0] * image[0] + basis[1] * image[1], axis=(1, 2))
        imag_part = jnp.sum(basis[0] * image[1] - basis[1] * image[0], axis=(1, 2))
        stacked.append(jnp.stack([real_part, imag_part]))
    return jnp.stack(stacked)


def local_squares(field):
    return jnp.sum(field[0] * field[0] + field[1] * field[1], axis=(1, 2))


def scaled(factor, field):
    real_f = factor[0][:, None, None]
    imag_f = factor[1][:, None, None]
    return jnp.stack([real_f * field[0] - imag_f * field[1], real_f * field[1] + imag_f * field[0]])


def shards(
    right_side, near_blocks, near_cols, partner, source_basis, target_basis, coupling, far_ranks
):
    rows = right_side.shape[3]
    total = float(rows * lax.axis_size("dom") * lax.axis_size("blk"))

    def operator(field):
        return apply_operator(
            field, near_blocks, near_cols, partner, source_basis, target_basis, coupling, far_ranks
        )

    start_sum = lax.psum(local_squares(right_side), ("dom", "blk"))
    beta = jnp.sqrt(start_sum / total + EPSILON)
    first_vec = right_side / beta[None, :, None, None]
    image_one = operator(first_vec)

    def projections(vectors, image):
        return lax.psum(local_products(vectors, image), ("dom", "blk")) / total

    def lengths(field):
        return lax.psum(local_squares(field), ("dom", "blk")) / total

    h_one_one = projections([first_vec], image_one)[0]
    rest_one = image_one - scaled(h_one_one, first_vec)
    h_two_one = jnp.sqrt(lengths(rest_one) + EPSILON)
    second_basis = rest_one / h_two_one[None, :, None, None]
    image_two = operator(second_basis)
    both = projections([first_vec, second_basis], image_two)
    h_one_two = both[0]
    h_two_two = both[1]
    rest_two = image_two - scaled(h_one_two, first_vec) - scaled(h_two_two, second_basis)
    h_three_two = jnp.sqrt(lengths(rest_two) + EPSILON)
    third_basis = rest_two / h_three_two[None, :, None, None]
    hessenberg = jnp.stack(
        [
            beta,
            h_one_one[0],
            h_one_one[1],
            h_two_one,
            h_one_two[0],
            h_one_two[1],
            h_two_two[0],
            h_two_two[1],
            h_three_two,
        ],
        axis=1,
    )
    return (second_basis, third_basis, hessenberg)


def solution(mesh):
    return jax.shard_map(
        shards,
        mesh=mesh,
        in_specs=(
            P(None, None, "dom", "blk"),
            P("dom", "blk", None, None, None, None),
            P("dom", "blk", None),
            P("dom", "blk"),
            P("dom", None, None, "blk"),
            P("dom", None, None, "blk"),
            P("dom", "blk", None, None, None, None),
            P("dom", "blk", None),
        ),
        out_specs=(P(None, None, "dom", "blk"), P(None, None, "dom", "blk"), P()),
        check_vma=False,
    )
```

profile of v0, /device:TPU:0, one launch (start us, length us, event | category | flops | bytes accessed | tf_op | source)
XLA Modules:
  0.0 278.6 jit_solution(17837477689193010791)
XLA Ops:
  0.6 0.0 copy-start
  0.6 0.0 copy-start.2
  0.7 0.0 copy-start.3
  0.7 0.0 copy-start.4
  0.7 1.0 add_reduce_fusion.3
  1.7 42.0 %psum.35 = f32[4]{0:T(128)S(1)} all-reduce(f32[4]{0:T(128)S(1)} %add_reduce_fusion.3), channel_id=1, replica_groups=mesh['dom'=2,'blk'=16] {'dom','blk'}, use_global_device_ids=true, to_apply=%region_1.0 | all-reduce | flops 4 | bytes 32 | tf_op jit(solution)/shard_map/psum | solution.py:107
  43.7 0.8 fusion.64
  44.5 1.3 collective-permute-start
  45.8 1.3 collective-permute-start.1
  47.1 1.1 convolution_bitcast_fusion.3
  48.2 24.1 %all-gather = f32[32,4,64]{2,1,0:T(4,128)S(1)} all-gather(f32[2,4,64]{2,1,0:T(4,128)S(1)} %pad_maximum_fusion.2), channel_id=2, replica_groups=mesh['dom'=2,'blk'=16] {'blk'}, dimensions={0}, use_global_device_ids=true | all-gather | bytes 34816 | tf_op jit(solution)/shard_map/all_gather | solution.py:62
  72.3 0.7 iota_compare_fusion
  73.0 0.2 and_convert_fusion
  73.2 2.6 fusion.12
  75.9 0.0 copy-start.1
  75.9 0.1 convolution_bitcast_fusion.1
  76.1 0.1 reshape_squeeze.4
  76.2 4.4 %all_gather.13 = f32[2,4,2,512]{3,1,0,2:T(4,128)S(1)} all-gather(f32[2,4,1,512]{3,1,0,2:T(4,128)S(1)} %get-tuple-element.28), channel_id=1, replica_groups=mesh['dom'=2,'blk'=16] {'dom'}, dimensions={2}, use_global_device_ids=true | all-gather | bytes 49152 | tf_op jit(solution)/shard_map/all_gather | solution.py:71
  80.7 0.6 gather_fusion.1
  81.3 0.1 select_bitcast_fusion.1
  81.5 0.0 collective-permute-done
  81.5 0.0 collective-permute-done.1
  81.5 0.6 gather_fusion
  82.1 0.1 broadcast_select_fusion.1
  82.2 0.7 fusion.4
  82.9 0.1 add_reduce_fusion.2
  83.1 36.9 %psum.36 = f32[1,2,4]{2,1,0:T(2,128)S(1)} all-reduce(f32[1,2,4]{2,1,0:T(2,128)S(1)} %maximum_bitcast_fusion.6), channel_id=1, replica_groups=mesh['dom'=2,'blk'=16] {'dom','blk'}, use_global_device_ids=true, to_apply=%region_4.7 | all-reduce | flops 8 | bytes 64 | tf_op jit(solution)/shard_map/psum | solution.py:113
  120.0 0.1 multiply_subtract_fusion.2
  120.1 0.1 fusion.34
  120.2 0.1 copy.136
  120.3 41.3 %psum.37 = f32[4]{0:T(128)S(1)} all-reduce(f32[4]{0:T(128)S(1)} %fusion.34), channel_id=1, replica_groups=mesh['dom'=2,'blk'=16] {'dom','blk'}, use_global_device_ids=true, to_apply=%region_6.9 | all-reduce | flops 4 | bytes 32 | tf_op jit(solution)/shard_map/psum | solution.py:116
  161.6 0.1 fusion.63
  161.7 0.1 convolution_bitcast_fusion.2
  161.9 20.6 %all-gather.1 = f32[32,4,64]{2,1,0:T(4,128)S(1)} all-gather(f32[2,4,64]{2,1,0:T(4,128)S(1)} %pad_maximum_fusion.3), channel_id=3, replica_groups=mesh['dom'=2,'blk'=16] {'blk'}, dimensions={0}, use_global_device_ids=true | all-gather | bytes 34816 | tf_op jit(solution)/shard_map/all_gather | solution.py:62
  182.5 2.6 fusion.10
  185.1 2.2 collective-permute-start.2
  187.4 1.3 collective-permute-start.3
  188.7 4.4 %all_gather.15 = f32[2,4,2,512]{3,1,0,2:T(4,128)S(1)} all-gather(f32[2,4,1,512]{3,1,0,2:T(4,128)S(1)} %get-tuple-element.26), channel_id=1, replica_groups=mesh['dom'=2,'blk'=16] {'dom'}, dimensions={2}, use_global_device_ids=true | all-gather | bytes 49152 | tf_op jit(solution)/shard_map/all_gather | solution.py:71
  193.2 0.6 gather_fusion.3
  193.8 0.1 select_bitcast_fusion
  193.9 0.1 convolution_bitcast_fusion
  194.0 0.6 copy.145
  194.7 0.1 copy.139
  194.8 0.0 collective-permute-done.2
  194.8 0.0 collective-permute-done.3
  194.8 0.6 gather_fusion.2
  195.4 0.1 broadcast_select_fusion
  195.5 0.7 fusion.7
  196.2 0.2 add_reduce_fusion.1
  196.4 0.1 copy.137
  196.5 39.3 %psum.38 = f32[2,2,4]{2,1,0:T(2,128)S(1)} all-reduce(f32[2,2,4]{2,1,0:T(2,128)S(1)} %pad_maximum_fusion.4), channel_id=1, replica_groups=mesh['dom'=2,'blk'=16] {'dom','blk'}, use_global_device_ids=true, to_apply=%region_11.14 | all-reduce | flops 16 | bytes 128 | tf_op jit(solution)/shard_map/psum | solution.py:113
  235.8 0.1 multiply_subtract_fusion
  235.9 0.1 multiply_subtract_fusion.1
  236.0 0.1 fusion.30
  236.1 0.1 copy.138
  236.2 40.5 %psum.39 = f32[4]{0:T(128)S(1)} all-reduce(f32[4]{0:T(128)S(1)} %fusion.30), channel_id=1, replica_groups=mesh['dom'=2,'blk'=16] {'dom','blk'}, use_global_device_ids=true, to_apply=%region_13.16 | all-reduce | flops 4 | bytes 32 | tf_op jit(solution)/shard_map/psum | solution.py:116
  276.7 0.1 copy.144
  276.8 0.1 copy.140
  276.9 0.1 copy.141
  277.0 0.1 copy.142
  277.1 0.1 copy.143
  277.2 0.1 broadcast_divide_fusion
  277.3 0.6 copy.146
  277.9 0.7 stack.135
  (56 shorter events, 0.5 us)
Async XLA Ops:
  0.6 81.5 %copy-start = (bf16[1,2,4,2,256,256]{5,4,3,2,1,0:T(8,128)(2,1)S(1)}, bf16[1,2,4,2,256,256]{5,4,3,2,1,0:T(8,128)(2,1)}, u32[]{:S(2)}) copy-start(bf16[1,2,4,2,256,256]{5,4,3,2,1,0:T(8,128)(2,1)} %param.13) | copy-start | bytes 6291460
  0.6 75.3 %copy-start.2 = (bf16[1,2,64,512]{3,2,1,0:T(8,128)(2,1)S(1)}, bf16[1,2,64,512]{3,2,1,0:T(8,128)(2,1)}, u32[]{:S(2)}) copy-start(bf16[1,2,64,512]{3,2,1,0:T(8,128)(2,1)} %param.17) | copy-start | bytes 393220
  0.7 75.4 %copy-start.3 = (s32[1,2,4]{2,1,0:T(2,128)S(1)}, s32[1,2,4]{2,1,0:T(2,128)}, u32[]{:S(2)}) copy-start(s32[1,2,4]{2,1,0:T(2,128)} %param.14) | copy-start | bytes 100
  0.7 75.5 %copy-start.4 = (s32[1,2]{1,0:T(1,128)S(1)}, s32[1,2]{1,0:T(1,128)}, u32[]{:S(2)}) copy-start(s32[1,2]{1,0:T(1,128)} %param.15) | copy-start | bytes 28
  44.5 37.0 %collective-permute-start = (bf16[2,4,1,512]{3,1,0,2:T(4,128)(2,1)S(1)}, bf16[2,4,1,512]{3,1,0,2:T(4,128)(2,1)S(1)}, u32[]{:S(2)}, u32[]{:S(2)}) collective-permute-start(bf16[2,4,1,512]{3,1,0,2:T(4,128)(2,1)S(1)} %get-tuple-element.27), channel_id=1, source_target_pairs={{0,1},{1,2},{2,3},{3,4},{4,5},{5,6},{6,7},{7,8},{8,9},{9,10},{10,1... | collective-permute-start | bytes 24584 | tf_op jit(solution)/shard_map/ppermute | solution.py:17
  45.8 35.7 %collective-permute-start.1 = (bf16[2,4,1,512]{3,1,0,2:T(4,128)(2,1)S(1)}, bf16[2,4,1,512]{3,1,0,2:T(4,128)(2,1)S(1)}, u32[]{:S(2)}, u32[]{:S(2)}) collective-permute-start(bf16[2,4,1,512]{3,1,0,2:T(4,128)(2,1)S(1)} %get-tuple-element.27), channel_id=1, source_target_pairs={{1,0},{2,1},{3,2},{4,3},{5,4},{6,5},{7,6},{8,7},{9,8},{10,9},{11,1... | collective-permute-start | bytes 24584 | tf_op jit(solution)/shard_map/ppermute | solution.py:19
  75.9 85.8 %copy-start.1 = (bf16[1,2,64,512]{3,2,1,0:T(8,128)(2,1)S(1)}, bf16[1,2,64,512]{3,2,1,0:T(8,128)(2,1)}, u32[]{:S(2)}) copy-start(bf16[1,2,64,512]{3,2,1,0:T(8,128)(2,1)} %param.16) | copy-start | bytes 393220
  185.1 9.7 %collective-permute-start.2 = (bf16[2,4,1,512]{3,1,0,2:T(4,128)(2,1)S(1)}, bf16[2,4,1,512]{3,1,0,2:T(4,128)(2,1)S(1)}, u32[]{:S(2)}, u32[]{:S(2)}) collective-permute-start(bf16[2,4,1,512]{3,1,0,2:T(4,128)(2,1)S(1)} %get-tuple-element.25), channel_id=1, source_target_pairs={{0,1},{1,2},{2,3},{3,4},{4,5},{5,6},{6,7},{7,8},{8,9},{9,10},{10,1... | collective-permute-start | bytes 24584 | tf_op jit(solution)/shard_map/ppermute | solution.py:17
  187.4 7.4 %collective-permute-start.3 = (bf16[2,4,1,512]{3,1,0,2:T(4,128)(2,1)S(1)}, bf16[2,4,1,512]{3,1,0,2:T(4,128)(2,1)S(1)}, u32[]{:S(2)}, u32[]{:S(2)}) collective-permute-start(bf16[2,4,1,512]{3,1,0,2:T(4,128)(2,1)S(1)} %get-tuple-element.25), channel_id=1, source_target_pairs={{1,0},{2,1},{3,2},{4,3},{5,4},{6,5},{7,6},{8,7},{9,8},{10,9},{11,1... | collective-permute-start | bytes 24584 | tf_op jit(solution)/shard_map/ppermute | solution.py:19
where the time goes:
time: 280 us; the launch traced here: 279 us
  blocking collectives  254 us (91%)
  matrix products  8.05 us (3%)
  starting transfers between devices  6.11 us (2%)
  local copies, waits for them, and re-layouts  5.44 us (2%)
  other arithmetic  4.26 us (2%)
    psum x2, blocking collectives, lengths(): return lax.psum(local_squares(field), ('dom', 'blk')) / total  81.9 us
    psum x2, blocking collectives, projections(): return lax.psum(local_products(vectors, image), ('dom', 'blk')) / total  76.2 us
    all_gather x2, blocking collectives, apply_operator(): lax.all_gather(coeffs[None], 'blk', axis=0, tiled=True)  44.7 us
    psum x1, blocking collectives, shards(): start_sum = lax.psum(local_squares(right_side), ('dom', 'blk'))  42 us
    all_gather x2, blocking collectives, apply_operator(): every = lax.all_gather(vector, 'dom', axis=2, tiled=True)  8.85 us
  transfers between devices with their start and end apart: 4, of which 0 were waited for; matrix products, arithmetic and copies ran while one was open for 3% of the time, Pallas kernels for 0%

commit v1 on v0

--- a/solution.py
+++ b/solution.py
@@ -4,6 +4,22 @@
 from jax.sharding import PartitionSpec as P
 
 EPSILON = 1e-06
+
+
+def product_in_turn(value, axis, dim, term):
+    size, index, rows = (lax.axis_size(axis), lax.axis_index(axis), value.shape[dim])
+    forward = [(i, (i + 1) % size) for i in range(size)]
+    downward = [(i, (i - 1) % size) for i in range(size)]
+    half = size // 2
+    from_left = from_right = value
+    total = term(value, index * rows)
+    for step in range(1, half + 1):
+        from_left = lax.ppermute(from_left, axis, forward)
+        if step < size - half:
+            from_right = lax.ppermute(from_right, axis, downward)
+            total = total + term(from_right, (index + step) % size * rows)
+        total = total + term(from_left, (index - step) % size * rows)
+    return total
 
 
 def extended(cells, sides, width):
@@ -56,11 +72,16 @@
     limit = row_ranks[:, None, None]
     keep = (levels[None, :, None] < limit) & (levels[None, None, :] < limit)
     weights = row_coupling * keep[:, None].astype(jnp.float32)
-    inner = jnp.einsum(
-        "sakl,spql->apqk",
-        weights,
-        lax.all_gather(coeffs[None], "blk", axis=0, tiled=True),
-        precision=lax.Precision.HIGHEST,
+    inner = product_in_turn(
+        coeffs[None],
+        "blk",
+        0,
+        lambda part, start: jnp.einsum(
+            "sakl,spql->apqk",
+            lax.dynamic_slice_in_dim(weights, start, part.shape[0], axis=0),
+            part,
+            precision=lax.Precision.HIGHEST,
+        ),
     )
     far_coef = complex_mix(inner)
     rounded_coef = far_coef.astype(jnp.bfloat16)

time: 280 us -> 326 us (1.16)
  starting transfers between devices: 6.11 us -> 66 us
  blocking collectives: 254 us -> 208 us
  waiting for transfers between devices: 0.01 us -> 24 us
  other arithmetic: 4.26 us -> 7.85 us
    ppermute x0 -> x30, starting transfers between devices: none -> 59.4 us  [the longest x14 58.7 us: product_in_turn(): from_right = lax.ppermute(from_right, axis, downward)]
    all_gather x2 -> x0, blocking collectives: 44.7 us -> none  [apply_operator(): lax.all_gather(coeffs[None], 'blk', axis=0, tiled=True)]
    ppermute x0 -> x30, waiting for transfers between devices: none -> 24 us  [the longest x16 22.5 us: product_in_turn(): from_left = lax.ppermute(from_left, axis, forward)]
    dot_general x2 -> x32, matrix products: 5.25 us -> 8.17 us  [apply_operator(): jnp.einsum('sakl,spql->apqk', lax.dynamic_slice_in_dim(weights, start, pa...]
  transfers between devices with their start and end apart: 4 -> 34, of which waited for: 0 -> 16; matrix products, arithmetic and copies ran while one was open for 3% -> 6% of each run, Pallas kernels for 0% -> 0%
where the time goes in v1:
time: 326 us; the launch traced here: 325 us
  blocking collectives  208 us (64%)
  starting transfers between devices  66 us (20%)
  waiting for transfers between devices  24 us (7%)
  matrix products  11 us (3%)
  other arithmetic  7.85 us (2%)
  local copies, waits for them, and re-layouts  6.14 us (2%)
    psum x2, blocking collectives, lengths(): return lax.psum(local_squares(field), ('dom', 'blk')) / total  83.6 us
    psum x2, blocking collectives, projections(): return lax.psum(local_products(vectors, image), ('dom', 'blk')) / total  73.7 us
    ppermute x14, starting transfers between devices, product_in_turn(): from_right = lax.ppermute(from_right, axis, downward)  58.7 us
    psum x1, blocking collectives, shards(): start_sum = lax.psum(local_squares(right_side), ('dom', 'blk'))  42 us
    ppermute x16, waiting for transfers between devices, product_in_turn(): from_left = lax.ppermute(from_left, axis, forward)  22.5 us
    all_gather x2, blocking collectives, apply_operator(): every = lax.all_gather(vector, 'dom', axis=2, tiled=True)  8.82 us
    dot_general x32, matrix products, apply_operator(): jnp.einsum('sakl,spql->apqk', lax.dynamic_slice_in_dim(weights, start, pa...  8.17 us
  transfers between devices with their start and end apart: 34, of which 16 were waited for; matrix products, arithmetic and copies ran while one was open for 6% of the time, Pallas kernels for 0%

profile of v1, /device:TPU:0, one launch (start us, length us, event | category | flops | bytes accessed | tf_op | source)
XLA Modules:
  0.0 324.9 jit_solution(12209842988067755331)
XLA Ops:
  0.6 1.0 add_reduce_fusion.3
  1.6 42.0 %psum.35 = f32[4]{0:T(128)S(1)} all-reduce(f32[4]{0:T(128)S(1)} %add_reduce_fusion.3), channel_id=1, replica_groups=mesh['dom'=2,'blk'=16] {'dom','blk'}, use_global_device_ids=true, to_apply=%region_1.0 | all-reduce | flops 4 | bytes 32 | tf_op jit(solution)/shard_map/psum | solution.py:128
  43.6 0.8 fusion.218
  44.4 1.1 convolution_bitcast_fusion.3
  45.5 1.7 collective-permute-start.2
  47.2 2.7 collective-permute-start
  50.0 1.3 collective-permute-start.1
  51.5 0.8 reshape_squeeze.4
  52.3 0.7 compare_select_fusion
  52.9 0.7 compare_and_fusion
  53.6 0.7 iota_compare_fusion
  54.3 1.0 and_convert_fusion
  55.3 4.4 %all_gather.6 = f32[2,4,2,512]{3,1,0,2:T(4,128)S(1)} all-gather(f32[2,4,1,512]{3,1,0,2:T(4,128)S(1)} %get-tuple-element.25), channel_id=1, replica_groups=mesh['dom'=2,'blk'=16] {'dom'}, dimensions={2}, use_global_device_ids=true | all-gather | bytes 49152 | tf_op jit(solution)/shard_map/all_gather | solution.py:92
  59.8 1.5 bitcast_multiply_fusion
  61.6 0.6 gather_fusion.1
  62.6 4.3 %collective-permute-start.4 = (f32[1,2,4,64]{3,2,1,0:T(4,128)S(1)}, f32[1,2,4,64]{3,2,1,0:T(4,128)S(1)}, u32[]{:S(2)}, u32[]{:S(2)}) collective-permute-start(f32[1,2,4,64]{3,2,1,0:T(4,128)S(1)} %collective-permute-done.2), channel_id=1, source_target_pairs={{0,15},{1,0},{2,1},{3,2},{4,3},{5,4},{6,5},{7,6},{8,7},{9,8},{10,9... | collective-permute-start | bytes 6152 | tf_op jit(solution)/shard_map/ppermute | solution.py:19
  67.2 0.3 convolution_add_fusion.16
  67.4 0.7 collective-permute-done.5
  68.5 4.5 %collective-permute-start.6 = (f32[1,2,4,64]{3,2,1,0:T(4,128)S(1)}, f32[1,2,4,64]{3,2,1,0:T(4,128)S(1)}, u32[]{:S(2)}, u32[]{:S(2)}) collective-permute-start(f32[1,2,4,64]{3,2,1,0:T(4,128)S(1)} %collective-permute-done.4), channel_id=1, source_target_pairs={{0,15},{1,0},{2,1},{3,2},{4,3},{5,4},{6,5},{7,6},{8,7},{9,8},{10,9... | collective-permute-start | bytes 6152 | tf_op jit(solution)/shard_map/ppermute | solution.py:19
  73.2 0.7 collective-permute-done.7
  74.3 4.4 %collective-permute-start.8 = (f32[1,2,4,64]{3,2,1,0:T(4,128)S(1)}, f32[1,2,4,64]{3,2,1,0:T(4,128)S(1)}, u32[]{:S(2)}, u32[]{:S(2)}) collective-permute-start(f32[1,2,4,64]{3,2,1,0:T(4,128)S(1)} %collective-permute-done.6), channel_id=1, source_target_pairs={{0,15},{1,0},{2,1},{3,2},{4,3},{5,4},{6,5},{7,6},{8,7},{9,8},{10,9... | collective-permute-start | bytes 6152 | tf_op jit(solution)/shard_map/ppermute | solution.py:19
  79.0 0.6 gather_fusion
  79.7 0.7 fusion.4
  80.4 0.3 fusion.50
  80.7 0.3 fusion.21
  81.0 4.5 %collective-permute-start.10 = (f32[1,2,4,64]{3,2,1,0:T(4,128)S(1)}, f32[1,2,4,64]{3,2,1,0:T(4,128)S(1)}, u32[]{:S(2)}, u32[]{:S(2)}) collective-permute-start(f32[1,2,4,64]{3,2,1,0:T(4,128)S(1)} %collective-permute-done.8), channel_id=1, source_target_pairs={{0,15},{1,0},{2,1},{3,2},{4,3},{5,4},{6,5},{7,6},{8,7},{9,8},{10,9... | collective-permute-start | bytes 6152 | tf_op jit(solution)/shard_map/ppermute | solution.py:19
  85.5 0.6 collective-permute-done.11
  86.4 0.4 collective-permute-done.10
  86.8 4.4 %collective-permute-start.12 = (f32[1,2,4,64]{3,2,1,0:T(4,128)S(1)}, f32[1,2,4,64]{3,2,1,0:T(4,128)S(1)}, u32[]{:S(2)}, u32[]{:S(2)}) collective-permute-start(f32[1,2,4,64]{3,2,1,0:T(4,128)S(1)} %collective-permute-done.10), channel_id=1, source_target_pairs={{0,15},{1,0},{2,1},{3,2},{4,3},{5,4},{6,5},{7,6},{8,7},{9,8},{10,9... | collective-permute-start | bytes 6152 | tf_op jit(solution)/shard_map/ppermute | solution.py:19
  91.5 0.4 collective-permute-done.13
  92.1 0.4 collective-permute-done.12
  92.6 4.4 %collective-permute-start.14 = (f32[1,2,4,64]{3,2,1,0:T(4,128)S(1)}, f32[1,2,4,64]{3,2,1,0:T(4,128)S(1)}, u32[]{:S(2)}, u32[]{:S(2)}) collective-permute-start(f32[1,2,4,64]{3,2,1,0:T(4,128)S(1)} %collective-permute-done.12), channel_id=1, source_target_pairs={{0,15},{1,0},{2,1},{3,2},{4,3},{5,4},{6,5},{7,6},{8,7},{9,8},{10,9... | collective-permute-start | bytes 6152 | tf_op jit(solution)/shard_map/ppermute | solution.py:19
  97.2 0.4 collective-permute-done.15
  97.9 0.4 collective-permute-done.14
  98.6 4.8 %collective-permute-done.16 = f32[1,2,4,64]{3,2,1,0:T(4,128)S(1)} collective-permute-done((f32[1,2,4,64]{3,2,1,0:T(4,128)S(1)}, f32[1,2,4,64]{3,2,1,0:T(4,128)S(1)}, u32[]{:S(2)}, u32[]{:S(2)}) %collective-permute-start.16) | collective-permute-done | bytes 2080 | tf_op jit(solution)/shard_map/ppermute | solution.py:17
  104.0 36.9 %psum.36 = f32[1,2,4]{2,1,0:T(2,128)S(1)} all-reduce(f32[1,2,4]{2,1,0:T(2,128)S(1)} %maximum_bitcast_fusion.6), channel_id=1, replica_groups=mesh['dom'=2,'blk'=16] {'dom','blk'}, use_global_device_ids=true, to_apply=%region_4.7 | all-reduce | flops 8 | bytes 64 | tf_op jit(solution)/shard_map/psum | solution.py:134
  141.2 41.4 %psum.37 = f32[4]{0:T(128)S(1)} all-reduce(f32[4]{0:T(128)S(1)} %fusion.118), channel_id=1, replica_groups=mesh['dom'=2,'blk'=16] {'dom','blk'}, use_global_device_ids=true, to_apply=%region_6.9 | all-reduce | flops 4 | bytes 32 | tf_op jit(solution)/shard_map/psum | solution.py:137
  182.9 1.3 collective-permute-start.18
  184.2 4.0 %collective-permute-start.19 = (f32[1,2,4,64]{3,2,1,0:T(4,128)S(1)}, f32[1,2,4,64]{3,2,1,0:T(4,128)S(1)}, u32[]{:S(2)}, u32[]{:S(2)}) collective-permute-start(f32[1,2,4,64]{3,2,1,0:T(4,128)S(1)} %fusion.188), channel_id=1, source_target_pairs={{0,15},{1,0},{2,1},{3,2},{4,3},{5,4},{6,5},{7,6},{8,7},{9,8},{10,9... | collective-permute-start | bytes 6152 | tf_op jit(solution)/shard_map/ppermute | solution.py:19
  188.2 4.4 %all_gather.7 = f32[2,4,2,512]{3,1,0,2:T(4,128)S(1)} all-gather(f32[2,4,1,512]{3,1,0,2:T(4,128)S(1)} %get-tuple-element.23), channel_id=1, replica_groups=mesh['dom'=2,'blk'=16] {'dom'}, dimensions={2}, use_global_device_ids=true | all-gather | bytes 49152 | tf_op jit(solution)/shard_map/all_gather | solution.py:92
  192.7 0.6 gather_fusion.3
  193.7 1.3 collective-permute-start.17
  195.0 0.6 copy.92
  195.8 4.4 %collective-permute-start.21 = (f32[1,2,4,64]{3,2,1,0:T(4,128)S(1)}, f32[1,2,4,64]{3,2,1,0:T(4,128)S(1)}, u32[]{:S(2)}, u32[]{:S(2)}) collective-permute-start(f32[1,2,4,64]{3,2,1,0:T(4,128)S(1)} %collective-permute-done.19), channel_id=1, source_target_pairs={{0,15},{1,0},{2,1},{3,2},{4,3},{5,4},{6,5},{7,6},{8,7},{9,8},{10,9... | collective-permute-start | bytes 6152 | tf_op jit(solution)/shard_map/ppermute | solution.py:19
  200.5 0.3 convolution_add_fusion.7
  200.8 5.5 %collective-permute-done.22 = f32[1,2,4,64]{3,2,1,0:T(4,128)S(1)} collective-permute-done((f32[1,2,4,64]{3,2,1,0:T(4,128)S(1)}, f32[1,2,4,64]{3,2,1,0:T(4,128)S(1)}, u32[]{:S(2)}, u32[]{:S(2)}) %collective-permute-start.22) | collective-permute-done | bytes 2080 | tf_op jit(solution)/shard_map/ppermute | solution.py:17
  206.6 4.4 %collective-permute-start.23 = (f32[1,2,4,64]{3,2,1,0:T(4,128)S(1)}, f32[1,2,4,64]{3,2,1,0:T(4,128)S(1)}, u32[]{:S(2)}, u32[]{:S(2)}) collective-permute-start(f32[1,2,4,64]{3,2,1,0:T(4,128)S(1)} %collective-permute-done.21), channel_id=1, source_target_pairs={{0,15},{1,0},{2,1},{3,2},{4,3},{5,4},{6,5},{7,6},{8,7},{9,8},{10,9... | collective-permute-start | bytes 6152 | tf_op jit(solution)/shard_map/ppermute | solution.py:19
  211.3 1.0 collective-permute-done.24
  212.6 4.4 %collective-permute-start.25 = (f32[1,2,4,64]{3,2,1,0:T(4,128)S(1)}, f32[1,2,4,64]{3,2,1,0:T(4,128)S(1)}, u32[]{:S(2)}, u32[]{:S(2)}) collective-permute-start(f32[1,2,4,64]{3,2,1,0:T(4,128)S(1)} %collective-permute-done.23), channel_id=1, source_target_pairs={{0,15},{1,0},{2,1},{3,2},{4,3},{5,4},{6,5},{7,6},{8,7},{9,8},{10,9... | collective-permute-start | bytes 6152 | tf_op jit(solution)/shard_map/ppermute | solution.py:19
  217.3 1.0 collective-permute-done.26
  218.6 4.4 %collective-permute-start.27 = (f32[1,2,4,64]{3,2,1,0:T(4,128)S(1)}, f32[1,2,4,64]{3,2,1,0:T(4,128)S(1)}, u32[]{:S(2)}, u32[]{:S(2)}) collective-permute-start(f32[1,2,4,64]{3,2,1,0:T(4,128)S(1)} %collective-permute-done.25), channel_id=1, source_target_pairs={{0,15},{1,0},{2,1},{3,2},{4,3},{5,4},{6,5},{7,6},{8,7},{9,8},{10,9... | collective-permute-start | bytes 6152 | tf_op jit(solution)/shard_map/ppermute | solution.py:19
  223.4 0.6 gather_fusion.2
  224.1 0.7 fusion.7
  224.8 0.3 fusion.42
  225.1 4.4 %collective-permute-start.29 = (f32[1,2,4,64]{3,2,1,0:T(4,128)S(1)}, f32[1,2,4,64]{3,2,1,0:T(4,128)S(1)}, u32[]{:S(2)}, u32[]{:S(2)}) collective-permute-start(f32[1,2,4,64]{3,2,1,0:T(4,128)S(1)} %collective-permute-done.27), channel_id=1, source_target_pairs={{0,15},{1,0},{2,1},{3,2},{4,3},{5,4},{6,5},{7,6},{8,7},{9,8},{10,9... | collective-permute-start | bytes 6152 | tf_op jit(solution)/shard_map/ppermute | solution.py:19
  229.8 1.0 collective-permute-done.30
  231.1 4.4 %collective-permute-start.31 = (f32[1,2,4,64]{3,2,1,0:T(4,128)S(1)}, f32[1,2,4,64]{3,2,1,0:T(4,128)S(1)}, u32[]{:S(2)}, u32[]{:S(2)}) collective-permute-start(f32[1,2,4,64]{3,2,1,0:T(4,128)S(1)} %collective-permute-done.29), channel_id=1, source_target_pairs={{0,15},{1,0},{2,1},{3,2},{4,3},{5,4},{6,5},{7,6},{8,7},{9,8},{10,9... | collective-permute-start | bytes 6152 | tf_op jit(solution)/shard_map/ppermute | solution.py:19
  235.8 1.0 collective-permute-done.32
  237.2 0.3 fusion.11
  237.5 5.4 %collective-permute-done.33 = f32[1,2,4,64]{3,2,1,0:T(4,128)S(1)} collective-permute-done((f32[1,2,4,64]{3,2,1,0:T(4,128)S(1)}, f32[1,2,4,64]{3,2,1,0:T(4,128)S(1)}, u32[]{:S(2)}, u32[]{:S(2)}) %collective-permute-start.33) | collective-permute-done | bytes 2080 | tf_op jit(solution)/shard_map/ppermute | solution.py:17
  243.6 36.8 %psum.38 = f32[2,2,4]{2,1,0:T(2,128)S(1)} all-reduce(f32[2,2,4]{2,1,0:T(2,128)S(1)} %pad_maximum_fusion.6), channel_id=1, replica_groups=mesh['dom'=2,'blk'=16] {'dom','blk'}, use_global_device_ids=true, to_apply=%region_11.14 | all-reduce | flops 16 | bytes 128 | tf_op jit(solution)/shard_map/psum | solution.py:134
  280.8 42.2 %psum.39 = f32[4]{0:T(128)S(1)} all-reduce(f32[4]{0:T(128)S(1)} %fusion.114), channel_id=1, replica_groups=mesh['dom'=2,'blk'=16] {'dom','blk'}, use_global_device_ids=true, to_apply=%region_13.16 | all-reduce | flops 4 | bytes 32 | tf_op jit(solution)/shard_map/psum | solution.py:137
  323.6 0.6 copy.93
  324.2 0.7 stack.135
  (137 shorter events, 10.6 us)
Async XLA Ops:
  0.6 79.1 %copy-start = (bf16[1,2,4,2,256,256]{5,4,3,2,1,0:T(8,128)(2,1)S(1)}, bf16[1,2,4,2,256,256]{5,4,3,2,1,0:T(8,128)(2,1)}, u32[]{:S(2)}) copy-start(bf16[1,2,4,2,256,256]{5,4,3,2,1,0:T(8,128)(2,1)} %param.13) | copy-start | bytes 6291460
  45.5 17.0 %collective-permute-start.2 = (f32[1,2,4,64]{3,2,1,0:T(4,128)S(1)}, f32[1,2,4,64]{3,2,1,0:T(4,128)S(1)}, u32[]{:S(2)}, u32[]{:S(2)}) collective-permute-start(f32[1,2,4,64]{3,2,1,0:T(4,128)S(1)} %fusion.189), channel_id=1, source_target_pairs={{0,15},{1,0},{2,1},{3,2},{4,3},{5,4},{6,5},{7,6},{8,7},{9,8},{10,9... | collective-permute-start | bytes 6152 | tf_op jit(solution)/shard_map/ppermute | solution.py:19
  47.2 15.2 %collective-permute-start.3 = (f32[1,2,4,64]{3,2,1,0:T(4,128)S(1)}, f32[1,2,4,64]{3,2,1,0:T(4,128)S(1)}, u32[]{:S(2)}, u32[]{:S(2)}) collective-permute-start(f32[1,2,4,64]{3,2,1,0:T(4,128)S(1)} %fusion.189), channel_id=1, source_target_pairs={{0,1},{1,2},{2,3},{3,4},{4,5},{5,6},{6,7},{7,8},{8,9},{9,10},{10,1... | collective-permute-start | bytes 6152 | tf_op jit(solution)/shard_map/ppermute | solution.py:17
  47.2 31.8 %collective-permute-start = (bf16[2,4,1,512]{3,1,0,2:T(4,128)(2,1)S(1)}, bf16[2,4,1,512]{3,1,0,2:T(4,128)(2,1)S(1)}, u32[]{:S(2)}, u32[]{:S(2)}) collective-permute-start(bf16[2,4,1,512]{3,1,0,2:T(4,128)(2,1)S(1)} %get-tuple-element.24), channel_id=1, source_target_pairs={{0,1},{1,2},{2,3},{3,4},{4,5},{5,6},{6,7},{7,8},{8,9},{9,10},{10,1... | collective-permute-start | bytes 24584 | tf_op jit(solution)/shard_map/ppermute | solution.py:33
  50.0 29.0 %collective-permute-start.1 = (bf16[2,4,1,512]{3,1,0,2:T(4,128)(2,1)S(1)}, bf16[2,4,1,512]{3,1,0,2:T(4,128)(2,1)S(1)}, u32[]{:S(2)}, u32[]{:S(2)}) collective-permute-start(bf16[2,4,1,512]{3,1,0,2:T(4,128)(2,1)S(1)} %get-tuple-element.24), channel_id=1, source_target_pairs={{1,0},{2,1},{3,2},{4,3},{5,4},{6,5},{7,6},{8,7},{9,8},{10,9},{11,1... | collective-permute-start | bytes 24584 | tf_op jit(solution)/shard_map/ppermute | solution.py:35
  61.3 42.4 %copy-start.2 = (bf16[1,2,64,512]{3,2,1,0:T(8,128)(2,1)S(1)}, bf16[1,2,64,512]{3,2,1,0:T(8,128)(2,1)}, u32[]{:S(2)}) copy-start(bf16[1,2,64,512]{3,2,1,0:T(8,128)(2,1)} %param.17) | copy-start | bytes 393220
  62.4 5.8 %collective-permute-start.5 = (f32[1,2,4,64]{3,2,1,0:T(4,128)S(1)}, f32[1,2,4,64]{3,2,1,0:T(4,128)S(1)}, u32[]{:S(2)}, u32[]{:S(2)}) collective-permute-start(f32[1,2,4,64]{3,2,1,0:T(4,128)S(1)} %collective-permute-done.3), channel_id=1, source_target_pairs={{0,1},{1,2},{2,3},{3,4},{4,5},{5,6},{6,7},{7,8},{8,9},{9,10},{10,1... | collective-permute-start | bytes 6152 | tf_op jit(solution)/shard_map/ppermute | solution.py:17
  62.6 5.9 %collective-permute-start.4 = (f32[1,2,4,64]{3,2,1,0:T(4,128)S(1)}, f32[1,2,4,64]{3,2,1,0:T(4,128)S(1)}, u32[]{:S(2)}, u32[]{:S(2)}) collective-permute-start(f32[1,2,4,64]{3,2,1,0:T(4,128)S(1)} %collective-permute-done.2), channel_id=1, source_target_pairs={{0,15},{1,0},{2,1},{3,2},{4,3},{5,4},{6,5},{7,6},{8,7},{9,8},{10,9... | collective-permute-start | bytes 6152 | tf_op jit(solution)/shard_map/ppermute | solution.py:19
  67.1 115.6 %copy-start.1 = (bf16[1,2,64,512]{3,2,1,0:T(8,128)(2,1)S(1)}, bf16[1,2,64,512]{3,2,1,0:T(8,128)(2,1)}, u32[]{:S(2)}) copy-start(bf16[1,2,64,512]{3,2,1,0:T(8,128)(2,1)} %param.16) | copy-start | bytes 393220
  68.2 5.7 %collective-permute-start.7 = (f32[1,2,4,64]{3,2,1,0:T(4,128)S(1)}, f32[1,2,4,64]{3,2,1,0:T(4,128)S(1)}, u32[]{:S(2)}, u32[]{:S(2)}) collective-permute-start(f32[1,2,4,64]{3,2,1,0:T(4,128)S(1)} %collective-permute-done.5), channel_id=1, source_target_pairs={{0,1},{1,2},{2,3},{3,4},{4,5},{5,6},{6,7},{7,8},{8,9},{9,10},{10,1... | collective-permute-start | bytes 6152 | tf_op jit(solution)/shard_map/ppermute | solution.py:17
  68.5 5.8 %collective-permute-start.6 = (f32[1,2,4,64]{3,2,1,0:T(4,128)S(1)}, f32[1,2,4,64]{3,2,1,0:T(4,128)S(1)}, u32[]{:S(2)}, u32[]{:S(2)}) collective-permute-start(f32[1,2,4,64]{3,2,1,0:T(4,128)S(1)} %collective-permute-done.4), channel_id=1, source_target_pairs={{0,15},{1,0},{2,1},{3,2},{4,3},{5,4},{6,5},{7,6},{8,7},{9,8},{10,9... | collective-permute-start | bytes 6152 | tf_op jit(solution)/shard_map/ppermute | solution.py:19
  73.9 6.5 %collective-permute-start.9 = (f32[1,2,4,64]{3,2,1,0:T(4,128)S(1)}, f32[1,2,4,64]{3,2,1,0:T(4,128)S(1)}, u32[]{:S(2)}, u32[]{:S(2)}) collective-permute-start(f32[1,2,4,64]{3,2,1,0:T(4,128)S(1)} %collective-permute-done.7), channel_id=1, source_target_pairs={{0,1},{1,2},{2,3},{3,4},{4,5},{5,6},{6,7},{7,8},{8,9},{9,10},{10,1... | collective-permute-start | bytes 6152 | tf_op jit(solution)/shard_map/ppermute | solution.py:17
  74.3 6.4 %collective-permute-start.8 = (f32[1,2,4,64]{3,2,1,0:T(4,128)S(1)}, f32[1,2,4,64]{3,2,1,0:T(4,128)S(1)}, u32[]{:S(2)}, u32[]{:S(2)}) collective-permute-start(f32[1,2,4,64]{3,2,1,0:T(4,128)S(1)} %collective-permute-done.6), channel_id=1, source_target_pairs={{0,15},{1,0},{2,1},{3,2},{4,3},{5,4},{6,5},{7,6},{8,7},{9,8},{10,9... | collective-permute-start | bytes 6152 | tf_op jit(solution)/shard_map/ppermute | solution.py:19
  80.4 5.8 %collective-permute-start.11 = (f32[1,2,4,64]{3,2,1,0:T(4,128)S(1)}, f32[1,2,4,64]{3,2,1,0:T(4,128)S(1)}, u32[]{:S(2)}, u32[]{:S(2)}) collective-permute-start(f32[1,2,4,64]{3,2,1,0:T(4,128)S(1)} %collective-permute-done.9), channel_id=1, source_target_pairs={{0,1},{1,2},{2,3},{3,4},{4,5},{5,6},{6,7},{7,8},{8,9},{9,10},{10,1... | collective-permute-start | bytes 6152 | tf_op jit(solution)/shard_map/ppermute | solution.py:17
  81.0 5.8 %collective-permute-start.10 = (f32[1,2,4,64]{3,2,1,0:T(4,128)S(1)}, f32[1,2,4,64]{3,2,1,0:T(4,128)S(1)}, u32[]{:S(2)}, u32[]{:S(2)}) collective-permute-start(f32[1,2,4,64]{3,2,1,0:T(4,128)S(1)} %collective-permute-done.8), channel_id=1, source_target_pairs={{0,15},{1,0},{2,1},{3,2},{4,3},{5,4},{6,5},{7,6},{8,7},{9,8},{10,9... | collective-permute-start | bytes 6152 | tf_op jit(solution)/shard_map/ppermute | solution.py:19
  86.2 5.7 %collective-permute-start.13 = (f32[1,2,4,64]{3,2,1,0:T(4,128)S(1)}, f32[1,2,4,64]{3,2,1,0:T(4,128)S(1)}, u32[]{:S(2)}, u32[]{:S(2)}) collective-permute-start(f32[1,2,4,64]{3,2,1,0:T(4,128)S(1)} %collective-permute-done.11), channel_id=1, source_target_pairs={{0,1},{1,2},{2,3},{3,4},{4,5},{5,6},{6,7},{7,8},{8,9},{9,10},{10,1... | collective-permute-start | bytes 6152 | tf_op jit(solution)/shard_map/ppermute | solution.py:17
  86.8 5.7 %collective-permute-start.12 = (f32[1,2,4,64]{3,2,1,0:T(4,128)S(1)}, f32[1,2,4,64]{3,2,1,0:T(4,128)S(1)}, u32[]{:S(2)}, u32[]{:S(2)}) collective-permute-start(f32[1,2,4,64]{3,2,1,0:T(4,128)S(1)} %collective-permute-done.10), channel_id=1, source_target_pairs={{0,15},{1,0},{2,1},{3,2},{4,3},{5,4},{6,5},{7,6},{8,7},{9,8},{10,9... | collective-permute-start | bytes 6152 | tf_op jit(solution)/shard_map/ppermute | solution.py:19
  91.9 5.7 %collective-permute-start.15 = (f32[1,2,4,64]{3,2,1,0:T(4,128)S(1)}, f32[1,2,4,64]{3,2,1,0:T(4,128)S(1)}, u32[]{:S(2)}, u32[]{:S(2)}) collective-permute-start(f32[1,2,4,64]{3,2,1,0:T(4,128)S(1)} %collective-permute-done.13), channel_id=1, source_target_pairs={{0,1},{1,2},{2,3},{3,4},{4,5},{5,6},{6,7},{7,8},{8,9},{9,10},{10,1... | collective-permute-start | bytes 6152 | tf_op jit(solution)/shard_map/ppermute | solution.py:17
  92.6 5.7 %collective-permute-start.14 = (f32[1,2,4,64]{3,2,1,0:T(4,128)S(1)}, f32[1,2,4,64]{3,2,1,0:T(4,128)S(1)}, u32[]{:S(2)}, u32[]{:S(2)}) collective-permute-start(f32[1,2,4,64]{3,2,1,0:T(4,128)S(1)} %collective-permute-done.12), channel_id=1, source_target_pairs={{0,15},{1,0},{2,1},{3,2},{4,3},{5,4},{6,5},{7,6},{8,7},{9,8},{10,9... | collective-permute-start | bytes 6152 | tf_op jit(solution)/shard_map/ppermute | solution.py:19
  97.6 5.7 %collective-permute-start.16 = (f32[1,2,4,64]{3,2,1,0:T(4,128)S(1)}, f32[1,2,4,64]{3,2,1,0:T(4,128)S(1)}, u32[]{:S(2)}, u32[]{:S(2)}) collective-permute-start(f32[1,2,4,64]{3,2,1,0:T(4,128)S(1)} %collective-permute-done.15), channel_id=1, source_target_pairs={{0,1},{1,2},{2,3},{3,4},{4,5},{5,6},{6,7},{7,8},{8,9},{9,10},{10,1... | collective-permute-start | bytes 6152 | tf_op jit(solution)/shard_map/ppermute | solution.py:17
  182.9 40.5 %collective-permute-start.18 = (bf16[2,4,1,512]{3,1,0,2:T(4,128)(2,1)S(1)}, bf16[2,4,1,512]{3,1,0,2:T(4,128)(2,1)S(1)}, u32[]{:S(2)}, u32[]{:S(2)}) collective-permute-start(bf16[2,4,1,512]{3,1,0,2:T(4,128)(2,1)S(1)} %get-tuple-element.22), channel_id=1, source_target_pairs={{1,0},{2,1},{3,2},{4,3},{5,4},{6,5},{7,6},{8,7},{9,8},{10,9},{11,1... | collective-permute-start | bytes 24584 | tf_op jit(solution)/shard_map/ppermute | solution.py:35
  184.2 11.6 %collective-permute-start.19 = (f32[1,2,4,64]{3,2,1,0:T(4,128)S(1)}, f32[1,2,4,64]{3,2,1,0:T(4,128)S(1)}, u32[]{:S(2)}, u32[]{:S(2)}) collective-permute-start(f32[1,2,4,64]{3,2,1,0:T(4,128)S(1)} %fusion.188), channel_id=1, source_target_pairs={{0,15},{1,0},{2,1},{3,2},{4,3},{5,4},{6,5},{7,6},{8,7},{9,8},{10,9... | collective-permute-start | bytes 6152 | tf_op jit(solution)/shard_map/ppermute | solution.py:19
  193.6 6.8 %collective-permute-start.20 = (f32[1,2,4,64]{3,2,1,0:T(4,128)S(1)}, f32[1,2,4,64]{3,2,1,0:T(4,128)S(1)}, u32[]{:S(2)}, u32[]{:S(2)}) collective-permute-start(f32[1,2,4,64]{3,2,1,0:T(4,128)S(1)} %fusion.188), channel_id=1, source_target_pairs={{0,1},{1,2},{2,3},{3,4},{4,5},{5,6},{6,7},{7,8},{8,9},{9,10},{10,1... | collective-permute-start | bytes 6152 | tf_op jit(solution)/shard_map/ppermute | solution.py:17
  193.7 29.6 %collective-permute-start.17 = (bf16[2,4,1,512]{3,1,0,2:T(4,128)(2,1)S(1)}, bf16[2,4,1,512]{3,1,0,2:T(4,128)(2,1)S(1)}, u32[]{:S(2)}, u32[]{:S(2)}) collective-permute-start(bf16[2,4,1,512]{3,1,0,2:T(4,128)(2,1)S(1)} %get-tuple-element.22), channel_id=1, source_target_pairs={{0,1},{1,2},{2,3},{3,4},{4,5},{5,6},{6,7},{7,8},{8,9},{9,10},{10,1... | collective-permute-start | bytes 24584 | tf_op jit(solution)/shard_map/ppermute | solution.py:33
  195.8 10.8 %collective-permute-start.21 = (f32[1,2,4,64]{3,2,1,0:T(4,128)S(1)}, f32[1,2,4,64]{3,2,1,0:T(4,128)S(1)}, u32[]{:S(2)}, u32[]{:S(2)}) collective-permute-start(f32[1,2,4,64]{3,2,1,0:T(4,128)S(1)} %collective-permute-done.19), channel_id=1, source_target_pairs={{0,15},{1,0},{2,1},{3,2},{4,3},{5,4},{6,5},{7,6},{8,7},{9,8},{10,9... | collective-permute-start | bytes 6152 | tf_op jit(solution)/shard_map/ppermute | solution.py:19
  200.5 5.8 %collective-permute-start.22 = (f32[1,2,4,64]{3,2,1,0:T(4,128)S(1)}, f32[1,2,4,64]{3,2,1,0:T(4,128)S(1)}, u32[]{:S(2)}, u32[]{:S(2)}) collective-permute-start(f32[1,2,4,64]{3,2,1,0:T(4,128)S(1)} %collective-permute-done.20), channel_id=1, source_target_pairs={{0,1},{1,2},{2,3},{3,4},{4,5},{5,6},{6,7},{7,8},{8,9},{9,10},{10,1... | collective-permute-start | bytes 6152 | tf_op jit(solution)/shard_map/ppermute | solution.py:17
  206.5 5.8 %collective-permute-start.24 = (f32[1,2,4,64]{3,2,1,0:T(4,128)S(1)}, f32[1,2,4,64]{3,2,1,0:T(4,128)S(1)}, u32[]{:S(2)}, u32[]{:S(2)}) collective-permute-start(f32[1,2,4,64]{3,2,1,0:T(4,128)S(1)} %collective-permute-done.22), channel_id=1, source_target_pairs={{0,1},{1,2},{2,3},{3,4},{4,5},{5,6},{6,7},{7,8},{8,9},{9,10},{10,1... | collective-permute-start | bytes 6152 | tf_op jit(solution)/shard_map/ppermute | solution.py:17
  206.6 6.0 %collective-permute-start.23 = (f32[1,2,4,64]{3,2,1,0:T(4,128)S(1)}, f32[1,2,4,64]{3,2,1,0:T(4,128)S(1)}, u32[]{:S(2)}, u32[]{:S(2)}) collective-permute-start(f32[1,2,4,64]{3,2,1,0:T(4,128)S(1)} %collective-permute-done.21), channel_id=1, source_target_pairs={{0,15},{1,0},{2,1},{3,2},{4,3},{5,4},{6,5},{7,6},{8,7},{9,8},{10,9... | collective-permute-start | bytes 6152 | tf_op jit(solution)/shard_map/ppermute | solution.py:19
  212.5 5.8 %collective-permute-start.26 = (f32[1,2,4,64]{3,2,1,0:T(4,128)S(1)}, f32[1,2,4,64]{3,2,1,0:T(4,128)S(1)}, u32[]{:S(2)}, u32[]{:S(2)}) collective-permute-start(f32[1,2,4,64]{3,2,1,0:T(4,128)S(1)} %collective-permute-done.24), channel_id=1, source_target_pairs={{0,1},{1,2},{2,3},{3,4},{4,5},{5,6},{6,7},{7,8},{8,9},{9,10},{10,1... | collective-permute-start | bytes 6152 | tf_op jit(solution)/shard_map/ppermute | solution.py:17
  212.6 6.0 %collective-permute-start.25 = (f32[1,2,4,64]{3,2,1,0:T(4,128)S(1)}, f32[1,2,4,64]{3,2,1,0:T(4,128)S(1)}, u32[]{:S(2)}, u32[]{:S(2)}) collective-permute-start(f32[1,2,4,64]{3,2,1,0:T(4,128)S(1)} %collective-permute-done.23), channel_id=1, source_target_pairs={{0,15},{1,0},{2,1},{3,2},{4,3},{5,4},{6,5},{7,6},{8,7},{9,8},{10,9... | collective-permute-start | bytes 6152 | tf_op jit(solution)/shard_map/ppermute | solution.py:19
  218.6 6.2 %collective-permute-start.28 = (f32[1,2,4,64]{3,2,1,0:T(4,128)S(1)}, f32[1,2,4,64]{3,2,1,0:T(4,128)S(1)}, u32[]{:S(2)}, u32[]{:S(2)}) collective-permute-start(f32[1,2,4,64]{3,2,1,0:T(4,128)S(1)} %collective-permute-done.26), channel_id=1, source_target_pairs={{0,1},{1,2},{2,3},{3,4},{4,5},{5,6},{6,7},{7,8},{8,9},{9,10},{10,1... | collective-permute-start | bytes 6152 | tf_op jit(solution)/shard_map/ppermute | solution.py:17
  218.6 6.4 %collective-permute-start.27 = (f32[1,2,4,64]{3,2,1,0:T(4,128)S(1)}, f32[1,2,4,64]{3,2,1,0:T(4,128)S(1)}, u32[]{:S(2)}, u32[]{:S(2)}) collective-permute-start(f32[1,2,4,64]{3,2,1,0:T(4,128)S(1)} %collective-permute-done.25), channel_id=1, source_target_pairs={{0,15},{1,0},{2,1},{3,2},{4,3},{5,4},{6,5},{7,6},{8,7},{9,8},{10,9... | collective-permute-start | bytes 6152 | tf_op jit(solution)/shard_map/ppermute | solution.py:19
  225.0 5.8 %collective-permute-start.30 = (f32[1,2,4,64]{3,2,1,0:T(4,128)S(1)}, f32[1,2,4,64]{3,2,1,0:T(4,128)S(1)}, u32[]{:S(2)}, u32[]{:S(2)}) collective-permute-start(f32[1,2,4,64]{3,2,1,0:T(4,128)S(1)} %collective-permute-done.28), channel_id=1, source_target_pairs={{0,1},{1,2},{2,3},{3,4},{4,5},{5,6},{6,7},{7,8},{8,9},{9,10},{10,1... | collective-permute-start | bytes 6152 | tf_op jit(solution)/shard_map/ppermute | solution.py:17
  225.1 6.0 %collective-permute-start.29 = (f32[1,2,4,64]{3,2,1,0:T(4,128)S(1)}, f32[1,2,4,64]{3,2,1,0:T(4,128)S(1)}, u32[]{:S(2)}, u32[]{:S(2)}) collective-permute-start(f32[1,2,4,64]{3,2,1,0:T(4,128)S(1)} %collective-permute-done.27), channel_id=1, source_target_pairs={{0,15},{1,0},{2,1},{3,2},{4,3},{5,4},{6,5},{7,6},{8,7},{9,8},{10,9... | collective-permute-start | bytes 6152 | tf_op jit(solution)/shard_map/ppermute | solution.py:19
  231.1 5.8 %collective-permute-start.32 = (f32[1,2,4,64]{3,2,1,0:T(4,128)S(1)}, f32[1,2,4,64]{3,2,1,0:T(4,128)S(1)}, u32[]{:S(2)}, u32[]{:S(2)}) collective-permute-start(f32[1,2,4,64]{3,2,1,0:T(4,128)S(1)} %collective-permute-done.30), channel_id=1, source_target_pairs={{0,1},{1,2},{2,3},{3,4},{4,5},{5,6},{6,7},{7,8},{8,9},{9,10},{10,1... | collective-permute-start | bytes 6152 | tf_op jit(solution)/shard_map/ppermute | solution.py:17
  231.1 6.0 %collective-permute-start.31 = (f32[1,2,4,64]{3,2,1,0:T(4,128)S(1)}, f32[1,2,4,64]{3,2,1,0:T(4,128)S(1)}, u32[]{:S(2)}, u32[]{:S(2)}) collective-permute-start(f32[1,2,4,64]{3,2,1,0:T(4,128)S(1)} %collective-permute-done.29), channel_id=1, source_target_pairs={{0,15},{1,0},{2,1},{3,2},{4,3},{5,4},{6,5},{7,6},{8,7},{9,8},{10,9... | collective-permute-start | bytes 6152 | tf_op jit(solution)/shard_map/ppermute | solution.py:19
  237.1 5.8 %collective-permute-start.33 = (f32[1,2,4,64]{3,2,1,0:T(4,128)S(1)}, f32[1,2,4,64]{3,2,1,0:T(4,128)S(1)}, u32[]{:S(2)}, u32[]{:S(2)}) collective-permute-start(f32[1,2,4,64]{3,2,1,0:T(4,128)S(1)} %collective-permute-done.32), channel_id=1, source_target_pairs={{0,1},{1,2},{2,3},{3,4},{4,5},{5,6},{6,7},{7,8},{8,9},{9,10},{10,1... | collective-permute-start | bytes 6152 | tf_op jit(solution)/shard_map/ppermute | solution.py:17
